TPU v7x, 32 devices: a whole 2x2x4 slice. The times are simulated.
32 devices in a mesh: seq: 8 (over y, x, core), rep: 4 (over z).
Axes of the slice: x: 2, y: 2, z: 4, core: 2. Of those that a mesh axis runs over, the one named last changes fastest.
Arguments:
- out_grad: bfloat16 [4, 16, 131072], P('rep', None, 'seq'), may hold values from -6 to 6
- gate_act: bfloat16 [4, 16, 131072], P('rep', None, 'seq'), may hold values from -6 to 6
- conv_out: bfloat16 [4, 16, 131072], P('rep', None, 'seq'), may hold values from -6 to 6
- value_act: bfloat16 [4, 16, 131072], P('rep', None, 'seq'), may hold values from -6 to 6
- filter_taps: float32 [131072], P('seq'), may hold values from -1 to 1
- skip_gain: float32 [16], replicated, may hold values from 0.25 to 1.75
Outputs:
- gate_grad: bfloat16 [4, 16, 131072], P('rep', None, 'seq')
- value_grad: bfloat16 [4, 16, 131072], P('rep', None, 'seq')
- filter_grad: float32 [131072], P('seq')
All inputs are finite; a program needn't handle non-finite values.
Results may differ from a plain program's by a relative error of at most 0.001.
Values sent between devices are 32-bit elements; how exact they have to be, the bound alone decides.
No kernel may reach another device: no remote copies, remote signals or barrier semaphores. Data moves between devices by JAX's collectives and lax.ppermute only.
A program may use at most 128 MiB of HBM per device.

v0:
```python
import math
import jax
import jax.numpy as jnp
from jax import lax
from jax.sharding import PartitionSpec as P

HIGHEST = lax.Precision.HIGHEST


def unit_table(product, modulus):
    phase_rad = (product % modulus).astype(jnp.float32) * (-2.0 * math.pi / modulus)
    return (jnp.cos(phase_rad), jnp.sin(phase_rad))


def middle_mix(table, values):
    lead_dims = values.shape[:-2]
    flat = values.reshape((-1,) + values.shape[-2:])
    tiled = jnp.broadcast_to(table[None], (flat.shape[0],) + table.shape)
    result = jnp.einsum("rka,rab->rkb", tiled, flat, precision=HIGHEST)
    return result.reshape(lead_dims + result.shape[-2:])


def middle_complex(left_re, left_im, table_re, table_im):
    out_re = middle_mix(table_re, left_re) - middle_mix(table_im, left_im)
    out_im = middle_mix(table_im, left_re) + middle_mix(table_re, left_im)
    return (out_re, out_im)


def last_complex(form, left_re, left_im, table_re, table_im):
    out_re = jnp.einsum(form, left_re, table_re, precision=HIGHEST) - jnp.einsum(
        form, left_im, table_im, precision=HIGHEST
    )
    out_im = jnp.einsum(form, left_re, table_im, precision=HIGHEST) + jnp.einsum(
        form, left_im, table_re, precision=HIGHEST
    )
    return (out_re, out_im)


def row_order(seq_count):
    slot_ids = jnp.arange(2 * seq_count, dtype=jnp.int32)
    owner_dev = slot_ids // 2
    second = jnp.where(owner_dev == 0, seq_count, 2 * seq_count - owner_dev)
    return jnp.where(slot_ids % 2 == 0, owner_dev, second)


def cross_forward(pieces):
    seq_count = pieces.shape[1]
    block_len = pieces.shape[2]
    modulus = 2 * seq_count * seq_count * block_len
    freq_rows = row_order(seq_count)
    sources = jnp.arange(seq_count, dtype=jnp.int32)
    table_re, table_im = unit_table(freq_rows[:, None] * sources[None, :], 2 * seq_count)
    mixed_re = middle_mix(table_re, pieces)
    mixed_im = middle_mix(table_im, pieces)
    offsets = lax.axis_index("seq") * block_len + jnp.arange(block_len, dtype=jnp.int32)
    twist_re, twist_im = unit_table(freq_rows[:, None] * offsets[None, :], modulus)
    return (mixed_re * twist_re - mixed_im * twist_im, mixed_re * twist_im + mixed_im * twist_re)


def cross_inverse(operands):
    re_part, im_part = operands
    seq_count = re_part.shape[1] // 2
    block_len = re_part.shape[2]
    modulus = 2 * seq_count * seq_count * block_len
    freq_rows = row_order(seq_count)
    offsets = lax.axis_index("seq") * block_len + jnp.arange(block_len, dtype=jnp.int32)
    twist_re, twist_im = unit_table(freq_rows[:, None] * offsets[None, :], modulus)
    re_part, im_part = (
        re_part * twist_re + im_part * twist_im,
        im_part * twist_re - re_part * twist_im,
    )
    sources = jnp.arange(seq_count, dtype=jnp.int32)
    table_re, table_im = unit_table(sources[:, None] * freq_rows[None, :], 2 * seq_count)
    out_re = middle_mix(table_re, re_part) + middle_mix(table_im, im_part)
    return out_re


def local_forward(operands):
    re_part, im_part = operands
    lead_dims = re_part.shape[:-1]
    length_s = re_part.shape[-1]
    rows_a = length_s // 128
    re_part = re_part.reshape(lead_dims + (rows_a, 128))
    im_part = im_part.reshape(lead_dims + (rows_a, 128))
    steps_a = jnp.arange(rows_a, dtype=jnp.int32)
    steps_b = jnp.arange(128, dtype=jnp.int32)
    first_re, first_im = unit_table(steps_a[:, None] * steps_a[None, :], rows_a)
    re_part, im_part = middle_complex(re_part, im_part, first_re, first_im)
    twist_re, twist_im = unit_table(steps_a[:, None] * steps_b[None, :], length_s)
    re_part, im_part = (
        re_part * twist_re - im_part * twist_im,
        re_part * twist_im + im_part * twist_re,
    )
    last_re, last_im = unit_table(steps_b[:, None] * steps_b[None, :], 128)
    return last_complex("...kb,bl->...kl", re_part, im_part, last_re, last_im)


def local_inverse(re_part, im_part):
    lead_dims = re_part.shape[:-2]
    rows_a = re_part.shape[-2]
    length_s = rows_a * 128
    steps_a = jnp.arange(rows_a, dtype=jnp.int32)
    steps_b = jnp.arange(128, dtype=jnp.int32)
    last_re, last_im = unit_table(steps_b[:, None] * steps_b[None, :], 128)
    re_part, im_part = last_complex("...kl,bl->...kb", re_part, im_part, last_re, -last_im)
    twist_re, twist_im = unit_table(steps_a[:, None] * steps_b[None, :], length_s)
    re_part, im_part = (
        re_part * twist_re + im_part * twist_im,
        im_part * twist_re - re_part * twist_im,
    )
    first_re, first_im = unit_table(steps_a[:, None] * steps_a[None, :], rows_a)
    re_part, im_part = middle_complex(re_part, im_part, first_re, -first_im)
    return (re_part.reshape(lead_dims + (length_s,)), im_part.reshape(lead_dims + (length_s,)))


def local(out_grad, gate_act, conv_out, value_act, filter_taps, skip_gain):
    batch_rows = out_grad.shape[0]
    channels = out_grad.shape[1]
    length_s = out_grad.shape[2]
    seq_count = lax.axis_size("seq")
    row_total = batch_rows * channels
    gated_rows = out_grad.astype(jnp.float32) * gate_act.astype(jnp.float32)
    gate_grad = (out_grad.astype(jnp.float32) * conv_out.astype(jnp.float32)).astype(jnp.bfloat16)
    stacked = jnp.concatenate(
        [
            gated_rows.reshape(row_total, length_s),
            value_act.astype(jnp.float32).reshape(row_total, length_s),
            filter_taps.reshape(1, length_s),
        ],
        axis=0,
    )
    mixed_re, mixed_im = cross_forward(
        lax.all_to_all(
            stacked.reshape(2 * row_total + 1, 1, length_s),
            "seq",
            split_axis=2,
            concat_axis=1,
            tiled=True,
        )
    )
    spec_re, spec_im = local_forward(
        (
            lax.all_to_all(mixed_re, "seq", split_axis=1, concat_axis=2, tiled=True),
            lax.all_to_all(mixed_im, "seq", split_axis=1, concat_axis=2, tiled=True),
        )
    )
    grad_re = spec_re[:row_total]
    grad_im = spec_im[:row_total]
    value_re = spec_re[row_total : 2 * row_total]
    value_im = spec_im[row_total : 2 * row_total]
    filt_re = spec_re[2 * row_total]
    filt_im = spec_im[2 * row_total]
    carry_re = filt_re * grad_re + filt_im * grad_im
    carry_im = filt_re * grad_im - filt_im * grad_re
    lag_re = jnp.sum(grad_re * value_re + grad_im * value_im, axis=0)
    lag_im = jnp.sum(grad_im * value_re - grad_re * value_im, axis=0)
    lag_re, lag_im = lax.psum((lag_re, lag_im), "rep")
    back_re, back_im = local_inverse(
        jnp.concatenate([carry_re, lag_re[None]], axis=0),
        jnp.concatenate([carry_im, lag_im[None]], axis=0),
    )
    rows_out = cross_inverse(
        (
            lax.all_to_all(back_re, "seq", split_axis=2, concat_axis=1, tiled=True),
            lax.all_to_all(back_im, "seq", split_axis=2, concat_axis=1, tiled=True),
        )
    )
    rows_time = lax.all_to_all(rows_out, "seq", split_axis=1, concat_axis=2, tiled=True)
    rows_time = rows_time.reshape(row_total + 1, length_s) * (1.0 / (2 * seq_count * length_s))
    carried = rows_time[:row_total].reshape(batch_rows, channels, length_s)
    value_grad = (carried + skip_gain[None, :, None] * gated_rows).astype(jnp.bfloat16)
    lag_taps = rows_time[row_total]
    norm_scale = 1.0 / math.sqrt(
        batch_rows * lax.axis_size("rep") * channels * length_s * seq_count
    )
    filter_grad = lag_taps * norm_scale
    return (gate_grad, value_grad, filter_grad)


def solution(mesh):
    return jax.shard_map(
        local,
        mesh=mesh,
        in_specs=(
            P("rep", None, "seq"),
            P("rep", None, "seq"),
            P("rep", None, "seq"),
            P("rep", None, "seq"),
            P("seq"),
            P(),
        ),
        out_specs=(P("rep", None, "seq"), P("rep", None, "seq"), P("seq")),
        check_vma=False,
    )
```

profile of v0, /device:TPU:0, one launch (start us, length us, event | category | flops | bytes accessed | tf_op | source)
XLA Modules:
  0.0 709.1 jit_solution(3196688340106611680)
XLA Ops:
  9.8 4.8 copy.63
  15.1 74.5 %reduce = f32[16384,33]{1,0:T(8,128)} reduce(f32[16384,1,33]{2,1,0:T(1,128)} %bitcast.95, f32[]{:T(128)} %broadcast.616), dimensions={1}, to_apply=%bitcast.60.reduce_sub_computation | reduce | bytes 4325380
  89.6 11.2 %reshape.394 = f32[8,1,67584]{2,1,0:T(1,128)} reshape(f32[16384,33]{1,0:T(8,128)} %reduce) | data formatting | bytes 4325376
  100.7 5.3 all-to-all-start
  106.8 26.6 %all-to-all-done = f32[8,1,67584]{2,1,0:T(1,128)} async-done(((f32[8,1,67584]{2,1,0:T(1,128)}), f32[8,1,67584]{2,1,0:T(1,128)}, u32[]{:S(2)}, u32[]{:S(2)}) %all-to-all-start) | async-done | bytes 2162720 | tf_op jit(solution)/shard_map/all_to_all | solution.py:133
  133.4 7.4 %reduce.1 = f32[8,67584]{1,0:T(8,128)S(1)} reduce(f32[8,1,67584]{2,1,0:T(1,128)} %all-to-all-done, f32[]{:T(128)} %broadcast.616), dimensions={1}, to_apply=%all_to_all.64.reduce_sub_computation | reduce | bytes 4325380 | tf_op jit(solution)/shard_map/all_to_all | solution.py:133
  140.8 20.0 %reshape.395 = f32[16384,1,33]{2,1,0:T(1,128)} reshape(f32[8,67584]{1,0:T(8,128)S(1)} %reduce.1) | data formatting | bytes 4325376
  160.7 5.5 copy.78
  166.3 3.8 fusion.38
  170.1 6.4 multiply_add_fusion.1
  176.5 4.9 copy.67
  181.4 4.7 all-to-all-start.2
  186.1 7.1 %copy.65 = f32[33,16,2048]{2,0,1:T(8,128)} copy(f32[33,16,2048]{2,1,0:T(8,128)} %get-tuple-element.16) | data formatting | bytes 8650752 | tf_op jit(solution)/shard_map/sub | solution.py:57
  193.2 53.3 %all-to-all-done.2 = f32[33,16,2048]{2,0,1:T(8,128)} async-done(((f32[33,16,2048]{2,0,1:T(8,128)}), f32[33,16,2048]{2,0,1:T(8,128)}, u32[]{:S(2)}, u32[]{:S(2)}) %all-to-all-start.2) | async-done | bytes 4325408 | tf_op jit(solution)/shard_map/all_to_all | solution.py:144
  246.4 4.7 all-to-all-start.1
  252.0 7.0 copy.81
  259.0 5.3 reshape_reshape.9
  264.3 47.2 %all-to-all-done.1 = f32[33,16,2048]{2,0,1:T(8,128)} async-done(((f32[33,16,2048]{2,0,1:T(8,128)}), f32[33,16,2048]{2,0,1:T(8,128)}, u32[]{:S(2)}, u32[]{:S(2)}) %all-to-all-start.1) | async-done | bytes 4325408 | tf_op jit(solution)/shard_map/all_to_all | solution.py:143
  311.5 7.0 copy.82
  318.5 5.3 reshape_reshape.8
  323.8 6.2 fusion.7
  330.0 4.5 fusion.11
  334.5 4.6 convolution_subtract_fusion.1
  339.1 4.8 convolution_add_fusion.2
  343.9 4.2 fusion.19
  348.1 4.2 fusion.20
  352.3 4.5 convolution_add_fusion.1
  356.9 4.3 convolution_subtract_fusion
  364.6 35.4 %all-reduce.3.cloned.1.call-done = (f32[1,2,128,128]{3,2,1,0:T(8,128)}, f32[1,2,128,128]{3,2,1,0:T(8,128)}) async-done(((f32[1,2,128,128]{3,2,1,0:T(8,128)}, f32[1,2,128,128]{3,2,1,0:T(8,128)}), (f32[1,2,128,128]{3,2,1,0:T(8,128)}, f32[1,2,128,128]{3,2,1,0:T(8,128)})) %all-reduce.3.cloned.1.call-update) | async-done | bytes 262160 | tf_op jit(solution)/shard_map/psum | solution.py:157
  400.0 4.0 fusion.13
  409.0 4.3 multiply_subtract_fusion.2
  415.4 3.6 convolution_add_fusion.3
  419.0 3.7 add.234
  422.7 18.8 %copy.71 = f32[17,2,16384]{0,1,2:T(2,128)} copy(f32[17,2,16384]{2,1,0:T(2,128)} %add.234) | data formatting | bytes 4456448 | tf_op jit(solution)/shard_map/add | solution.py:25
  441.5 27.5 %reshape.396 = f32[8,1,69632]{2,1,0:T(1,128)} reshape(f32[16384,2,17]{2,1,0:T(2,128)} %bitcast.88) | data formatting | bytes 4456448
  469.0 4.5 all-to-all-start.4
  473.6 3.7 fusion.29
  483.7 15.1 %copy.69 = f32[17,2,16384]{0,1,2:T(2,128)} copy(f32[17,2,16384]{2,1,0:T(2,128)S(1)} %sub.82) | data formatting | bytes 4456448 | tf_op jit(solution)/shard_map/sub | solution.py:24
  498.8 27.5 %reshape.398 = f32[8,1,69632]{2,1,0:T(1,128)} reshape(f32[16384,2,17]{2,1,0:T(2,128)} %bitcast.89) | data formatting | bytes 4456448
  526.3 4.6 all-to-all-start.3
  530.9 7.6 %reduce.2 = f32[8,69632]{1,0:T(8,128)S(1)} reduce(f32[8,1,69632]{2,1,0:T(1,128)} %all-to-all-done.4, f32[]{:T(128)} %broadcast.616), dimensions={1}, to_apply=%all_to_all.76.reduce_sub_computation | reduce | bytes 4456452 | tf_op jit(solution)/shard_map/all_to_all | solution.py:165
  538.5 32.8 %reshape.397 = f32[16384,2,17]{2,1,0:T(2,128)} reshape(f32[8,69632]{1,0:T(8,128)S(1)} %reduce.2) | data formatting | bytes 4456448
  571.3 22.0 %copy.72 = f32[17,8,2,2048]{3,2,1,0:T(2,128)} copy(f32[17,8,2,2048]{0,2,3,1:T(2,128)} %bitcast.90) | data formatting | bytes 4456448 | tf_op jit(solution)/shard_map/all_to_all | solution.py:165
  596.4 8.9 %reduce.3 = f32[8,69632]{1,0:T(8,128)} reduce(f32[8,1,69632]{2,1,0:T(1,128)} %all-to-all-done.3, f32[]{:T(128)} %broadcast.616), dimensions={1}, to_apply=%all_to_all.72.reduce_sub_computation | reduce | bytes 4456452 | tf_op jit(solution)/shard_map/all_to_all | solution.py:164
  605.4 35.9 %reshape.399 = f32[16384,2,17]{2,1,0:T(2,128)} reshape(f32[8,69632]{1,0:T(8,128)} %reduce.3) | data formatting | bytes 4456448
  641.2 22.0 %copy.70 = f32[17,8,2,2048]{3,2,1,0:T(2,128)} copy(f32[17,8,2,2048]{0,2,3,1:T(2,128)} %bitcast.91) | data formatting | bytes 4456448 | tf_op jit(solution)/shard_map/all_to_all | solution.py:164
  663.2 4.0 all_to_all.75
  672.6 24.9 %all_to_all.87 = f32[17,8,2048]{2,0,1:T(8,128)S(1)} all-to-all(f32[17,8,2048]{2,0,1:T(8,128)S(1)} %copy.73), channel_id=1, replica_groups=mesh['seq'=8,'rep'=4] {'seq'}, dimensions={1} | all-to-all | bytes 2228224 | tf_op jit(solution)/shard_map/all_to_all | solution.py:168
  (62 shorter events, 34.6 us)
Async XLA Ops:
  7.2 2.5 copy-start.9
  100.7 32.6 %all-to-all-start = ((f32[8,1,67584]{2,1,0:T(1,128)}), f32[8,1,67584]{2,1,0:T(1,128)}, u32[]{:S(2)}, u32[]{:S(2)}) async-start(f32[8,1,67584]{2,1,0:T(1,128)} %reshape.394), calls=%async_computation | async-start | bytes 4325376 | tf_op jit(solution)/shard_map/all_to_all | solution.py:133
  181.4 65.0 %all-to-all-start.2 = ((f32[33,16,2048]{2,0,1:T(8,128)}), f32[33,16,2048]{2,0,1:T(8,128)}, u32[]{:S(2)}, u32[]{:S(2)}) async-start(f32[33,16,2048]{2,0,1:T(8,128)} %copy.67), calls=%async_computation.2 | async-start | bytes 10485760 | tf_op jit(solution)/shard_map/all_to_all | solution.py:144
  246.4 65.0 %all-to-all-start.1 = ((f32[33,16,2048]{2,0,1:T(8,128)}), f32[33,16,2048]{2,0,1:T(8,128)}, u32[]{:S(2)}, u32[]{:S(2)}) async-start(f32[33,16,2048]{2,0,1:T(8,128)} %copy.65), calls=%async_computation.1 | async-start | bytes 10485760 | tf_op jit(solution)/shard_map/all_to_all | solution.py:143
  251.1 148.8 %all-reduce.3.cloned.1.call-start = ((), (), s32[]{:S(2)}) async-start(), calls=%async_computation.6 | async-start | bytes 524288 | tf_op jit(solution)/shard_map/psum | solution.py:157
  323.8 6.2 copy-start
  323.8 10.7 %slice-start = ((s8[4325376]{0:T(1024)(128)(4,1)}), s8[4194304]{0:T(1024)(128)(4,1)S(1)}, s32[]{:S(2)}) async-start(s8[4325376]{0:T(1024)(128)(4,1)} %bitcast.92), calls=%async_computation.7 | async-start | bytes 8388608
  330.0 4.5 slice-start.1
  364.3 41.9 %copy-start.3 = (f32[16,2,128,128]{3,2,1,0:T(8,128)}, f32[16,2,128,128]{3,2,1,0:T(8,128)S(1)}, u32[]{:S(2)}) copy-start(f32[16,2,128,128]{3,2,1,0:T(8,128)S(1)} %get-tuple-element.13) | copy-start | bytes 6291460
  400.0 4.0 copy-start.4
  400.0 4.0 copy-start.8
  404.0 2.2 copy-start.7
  413.2 2.2 copy-start.2
  469.0 57.3 %all-to-all-start.4 = ((f32[8,1,69632]{2,1,0:T(1,128)}), f32[8,1,69632]{2,1,0:T(1,128)}, u32[]{:S(2)}, u32[]{:S(2)}) async-start(f32[8,1,69632]{2,1,0:T(1,128)} %reshape.396), calls=%async_computation.4 | async-start | bytes 4456448 | tf_op jit(solution)/shard_map/all_to_all | solution.py:165
  526.3 70.1 %all-to-all-start.3 = ((f32[8,1,69632]{2,1,0:T(1,128)}), f32[8,1,69632]{2,1,0:T(1,128)}, u32[]{:S(2)}, u32[]{:S(2)}) async-start(f32[8,1,69632]{2,1,0:T(1,128)} %reshape.398), calls=%async_computation.3 | async-start | bytes 4456448 | tf_op jit(solution)/shard_map/all_to_all | solution.py:164
  667.2 3.2 copy-start.1
  698.5 1.0 copy-start.5
  698.5 1.2 copy-start.6
  698.5 1.2 copy-start.10
Sparse Core Ops, SparseCore 0:
  364.5 35.4 all-reduce.2
where the time goes:
time: 718 us; the launch traced here: 709 us
  local copies, waits for them, and re-layouts  296 us (41%)
  waiting for transfers between devices  162 us (23%)
  other arithmetic  109 us (15%)
  matrix products  78.3 us (11%)
  blocking collectives  24.9 us (3%)
  starting transfers between devices  23.8 us (3%)
  between operations  14.8 us (2%)
    unnamed x33, local copies, waits for them, and re-layouts  156 us
    unnamed x2, other arithmetic  74.5 us
    all_to_all x1, waiting for transfers between devices, local(): lax.all_to_all(mixed_im, 'seq', split_axis=1, concat_axis=2, tiled=True)  53.3 us
    dot_general x12, matrix products, middle_mix(): result = jnp.einsum('rka,rab->rkb', tiled, flat, precision=HIGHEST)  48 us
    all_to_all x1, waiting for transfers between devices, local(): lax.all_to_all(mixed_re, 'seq', split_axis=1, concat_axis=2, tiled=True)  47.2 us
    psum x1, waiting for transfers between devices, local(): lag_re, lag_im = lax.psum((lag_re, lag_im), 'rep')  35.4 us
    all_to_all x1, waiting for transfers between devices, local(): lax.all_to_all(stacked.reshape(2 * row_total + 1, 1, length_s), 'seq', sp...  26.6 us
    all_to_all x2, local copies, waits for them, and re-layouts, local(): lax.all_to_all(back_re, 'seq', split_axis=2, concat_axis=1, tiled=True)  26 us
  transfers between devices with their start and end apart: 6, of which 4 were waited for; matrix products, arithmetic and copies ran while one was open for 19% of the time, Pallas kernels for 0%

commit v1 on v0

--- a/solution.py
+++ b/solution.py
@@ -159,10 +159,15 @@
         jnp.concatenate([carry_re, lag_re[None]], axis=0),
         jnp.concatenate([carry_im, lag_im[None]], axis=0),
     )
+
+    def answer_heads_up(buf, on_dim, axis_no):
+        part_now = jnp.stack(jnp.split(buf, lax.axis_size("seq"), on_dim))
+        return jnp.concatenate(lax.all_to_all(part_now, "seq", 0, 0), axis=axis_no)
+
     rows_out = cross_inverse(
         (
             lax.all_to_all(back_re, "seq", split_axis=2, concat_axis=1, tiled=True),
-            lax.all_to_all(back_im, "seq", split_axis=2, concat_axis=1, tiled=True),
+            answer_heads_up(back_im, 2, 1),
         )
     )
     rows_time = lax.all_to_all(rows_out, "seq", split_axis=1, concat_axis=2, tiled=True)

time: 718 us -> 644 us (0.90)
  local copies, waits for them, and re-layouts: 296 us -> 213 us
  waiting for transfers between devices: 162 us -> 183 us
  other arithmetic: 109 us -> 101 us
    unnamed x33 -> x40, local copies, waits for them, and re-layouts: 156 us -> 107 us
    all_to_all x2 -> x0, local copies, waits for them, and re-layouts: 25.1 us -> none  [local(): lax.all_to_all(back_im, 'seq', split_axis=2, concat_axis=1, tiled=True)]
    all_to_all x1, waiting for transfers between devices: 0.01 us -> 20.6 us  [local(): lax.all_to_all(back_re, 'seq', split_axis=2, concat_axis=1, tiled=True)]
    add x2 -> x1, local copies, waits for them, and re-layouts: 22.5 us -> 3.66 us  [middle_complex(): out_im = middle_mix(table_im, left_re) + middle_mix(table_re, left_im)]
    all_to_all x1 -> x0, other arithmetic: 7.57 us -> none  [local(): lax.all_to_all(back_im, 'seq', split_axis=2, concat_axis=1, tiled=True)]
    reshape x0 -> x2, local copies, waits for them, and re-layouts: none -> 7.43 us  [answer_heads_up(): return jnp.concatenate(lax.all_to_all(part_now, 'seq', 0, 0), axis=axis_no)]
    unnamed x2 -> x3, other arithmetic: 74.5 us -> 74.5 us
  transfers between devices with their start and end apart: 6 -> 6, of which waited for: 4 -> 5; matrix products, arithmetic and copies ran while one was open for 19% -> 13% of each run, Pallas kernels for 0% -> 0%
where the time goes in v1:
time: 644 us; the launch traced here: 637 us
  local copies, waits for them, and re-layouts  213 us (33%)
  waiting for transfers between devices  183 us (28%)
  other arithmetic  101 us (16%)
  matrix products  78.3 us (12%)
  starting transfers between devices  23.7 us (4%)
  blocking collectives  23.4 us (4%)
  between operations  14.7 us (2%)
    unnamed x40, local copies, waits for them, and re-layouts  107 us
    unnamed x3, other arithmetic  74.5 us
    all_to_all x1, waiting for transfers between devices, local(): lax.all_to_all(mixed_re, 'seq', split_axis=1, concat_axis=2, tiled=True)  53.2 us
    dot_general x12, matrix products, middle_mix(): result = jnp.einsum('rka,rab->rkb', tiled, flat, precision=HIGHEST)  47.9 us
    all_to_all x1, waiting for transfers between devices, local(): lax.all_to_all(mixed_im, 'seq', split_axis=1, concat_axis=2, tiled=True)  47.2 us
    psum x1, waiting for transfers between devices, local(): lag_re, lag_im = lax.psum((lag_re, lag_im), 'rep')  35.3 us
    all_to_all x1, waiting for transfers between devices, local(): lax.all_to_all(stacked.reshape(2 * row_total + 1, 1, length_s), 'seq', sp...  26.5 us
    all_to_all x2, local copies, waits for them, and re-layouts, local(): lax.all_to_all(back_re, 'seq', split_axis=2, concat_axis=1, tiled=True)  25.9 us
  transfers between devices with their start and end apart: 6, of which 5 were waited for; matrix products, arithmetic and copies ran while one was open for 13% of the time, Pallas kernels for 0%

profile of v1, /device:TPU:0, one launch (start us, length us, event | category | flops | bytes accessed | tf_op | source)
XLA Modules:
  0.0 637.0 jit_solution(2106435466900264622)
XLA Ops:
  9.8 4.8 copy.60
  15.1 74.5 %reduce = f32[16384,33]{1,0:T(8,128)} reduce(f32[16384,1,33]{2,1,0:T(1,128)} %bitcast.123, f32[]{:T(128)} %broadcast.616), dimensions={1}, to_apply=%bitcast.90.reduce_sub_computation | reduce | bytes 4325380
  89.6 11.2 %reshape.402 = f32[8,1,67584]{2,1,0:T(1,128)} reshape(f32[16384,33]{1,0:T(8,128)} %reduce) | data formatting | bytes 4325376
  100.8 5.4 all-to-all-start
  107.0 26.5 %all-to-all-done = f32[8,1,67584]{2,1,0:T(1,128)} async-done(((f32[8,1,67584]{2,1,0:T(1,128)}), f32[8,1,67584]{2,1,0:T(1,128)}, u32[]{:S(2)}, u32[]{:S(2)}) %all-to-all-start) | async-done | bytes 2162720 | tf_op jit(solution)/shard_map/all_to_all | solution.py:133
  133.4 7.4 %reduce.1 = f32[8,67584]{1,0:T(8,128)S(1)} reduce(f32[8,1,67584]{2,1,0:T(1,128)} %all-to-all-done, f32[]{:T(128)} %broadcast.616), dimensions={1}, to_apply=%all_to_all.54.reduce_sub_computation | reduce | bytes 4325380 | tf_op jit(solution)/shard_map/all_to_all | solution.py:133
  140.8 20.2 %reshape.403 = f32[16384,1,33]{2,1,0:T(1,128)} reshape(f32[8,67584]{1,0:T(8,128)S(1)} %reduce.1) | data formatting | bytes 4325376
  161.0 5.5 copy.74
  166.6 3.8 fusion.46
  170.4 6.3 multiply_add_fusion.1
  176.7 4.9 copy.62
  181.7 4.7 all-to-all-start.1
  186.4 7.1 %copy.64 = f32[33,16,2048]{2,0,1:T(8,128)} copy(f32[33,16,2048]{2,1,0:T(8,128)} %get-tuple-element.15) | data formatting | bytes 8650752 | tf_op jit(solution)/shard_map/add | solution.py:57
  193.5 53.2 %all-to-all-done.1 = f32[33,16,2048]{2,0,1:T(8,128)} async-done(((f32[33,16,2048]{2,0,1:T(8,128)}), f32[33,16,2048]{2,0,1:T(8,128)}, u32[]{:S(2)}, u32[]{:S(2)}) %all-to-all-start.1) | async-done | bytes 4325408 | tf_op jit(solution)/shard_map/all_to_all | solution.py:143
  246.7 4.7 all-to-all-start.2
  252.2 7.0 %copy.78 = f32[33,8,2,2048]{3,1,2,0:T(8,128)} copy(f32[33,8,2,2048]{3,0,2,1:T(8,128)} %bitcast.5) | data formatting | bytes 8650752 | tf_op jit(solution)/shard_map/all_to_all | solution.py:143
  259.2 5.3 reshape_reshape.8
  264.5 47.2 %all-to-all-done.2 = f32[33,16,2048]{2,0,1:T(8,128)} async-done(((f32[33,16,2048]{2,0,1:T(8,128)}), f32[33,16,2048]{2,0,1:T(8,128)}, u32[]{:S(2)}, u32[]{:S(2)}) %all-to-all-start.2) | async-done | bytes 4325408 | tf_op jit(solution)/shard_map/all_to_all | solution.py:144
  311.7 7.0 %copy.77 = f32[33,8,2,2048]{3,1,2,0:T(8,128)} copy(f32[33,8,2,2048]{3,0,2,1:T(8,128)} %bitcast.7) | data formatting | bytes 8650752 | tf_op jit(solution)/shard_map/all_to_all | solution.py:144
  318.7 5.3 reshape_reshape.9
  324.1 6.2 fusion.7
  330.4 4.4 fusion.11
  334.8 4.6 convolution_add_fusion.2
  339.4 4.8 convolution_subtract_fusion.1
  344.2 4.2 fusion.19
  348.4 4.2 fusion.20
  352.6 4.5 convolution_add_fusion.1
  357.1 4.3 convolution_subtract_fusion
  364.8 35.3 %all-reduce.3.cloned.1.call-done = (f32[1,2,128,128]{3,2,1,0:T(8,128)}, f32[1,2,128,128]{3,2,1,0:T(8,128)}) async-done(((f32[1,2,128,128]{3,2,1,0:T(8,128)}, f32[1,2,128,128]{3,2,1,0:T(8,128)}), (f32[1,2,128,128]{3,2,1,0:T(8,128)}, f32[1,2,128,128]{3,2,1,0:T(8,128)})) %all-reduce.3.cloned.1.call-update) | async-done | bytes 262160 | tf_op jit(solution)/shard_map/psum | solution.py:157
  400.2 4.0 fusion.13
  409.2 4.3 multiply_subtract_fusion.2
  415.7 3.6 convolution_add_fusion.3
  419.3 3.7 add.234
  436.4 4.5 all-to-all-start.4
  441.0 3.7 fusion.29
  444.7 3.5 convolution_subtract_fusion.2
  451.1 15.1 %copy.66 = f32[17,2,16384]{0,1,2:T(2,128)} copy(f32[17,2,16384]{2,1,0:T(2,128)S(1)} %sub.82) | data formatting | bytes 4456448 | tf_op jit(solution)/shard_map/sub | solution.py:24
  466.2 27.5 %reshape.404 = f32[8,1,69632]{2,1,0:T(1,128)} reshape(f32[16384,2,17]{2,1,0:T(2,128)} %bitcast.116) | data formatting | bytes 4456448
  493.7 4.4 all-to-all-start.3
  498.1 4.2 copy.68
  502.4 3.2 reshape.395
  505.6 20.6 %all-to-all-done.3 = f32[8,1,69632]{2,1,0:T(1,128)} async-done(((f32[8,1,69632]{2,1,0:T(1,128)}), f32[8,1,69632]{2,1,0:T(1,128)}, u32[]{:S(2)}, u32[]{:S(2)}) %all-to-all-start.3) | async-done | bytes 2228256 | tf_op jit(solution)/shard_map/all_to_all | solution.py:169
  526.1 9.0 %reduce.2 = f32[8,69632]{1,0:T(8,128)} reduce(f32[8,1,69632]{2,1,0:T(1,128)} %all-to-all-done.3, f32[]{:T(128)} %broadcast.616), dimensions={1}, to_apply=%all_to_all.62.reduce_sub_computation | reduce | bytes 4456452 | tf_op jit(solution)/shard_map/all_to_all | solution.py:169
  535.1 36.0 %reshape.405 = f32[16384,2,17]{2,1,0:T(2,128)} reshape(f32[8,69632]{1,0:T(8,128)} %reduce.2) | data formatting | bytes 4456448
  571.1 22.0 %copy.67 = f32[17,8,2,2048]{3,2,1,0:T(2,128)} copy(f32[17,8,2,2048]{0,2,3,1:T(2,128)} %bitcast.117) | data formatting | bytes 4456448 | tf_op jit(solution)/shard_map/all_to_all | solution.py:169
  593.1 3.9 all_to_all.65
  597.0 3.2 fusion.3
  602.5 23.4 %all_to_all.74 = f32[17,8,2048]{2,0,1:T(8,128)S(1)} all-to-all(f32[17,8,2048]{2,0,1:T(8,128)S(1)} %copy.69), channel_id=1, replica_groups=mesh['seq'=8,'rep'=4] {'seq'}, dimensions={1} | all-to-all | bytes 2228224 | tf_op jit(solution)/shard_map/all_to_all | solution.py:173
  (69 shorter events, 37.8 us)
Async XLA Ops:
  7.2 2.5 copy-start.8
  100.8 32.6 %all-to-all-start = ((f32[8,1,67584]{2,1,0:T(1,128)}), f32[8,1,67584]{2,1,0:T(1,128)}, u32[]{:S(2)}, u32[]{:S(2)}) async-start(f32[8,1,67584]{2,1,0:T(1,128)} %reshape.402), calls=%async_computation | async-start | bytes 4325376 | tf_op jit(solution)/shard_map/all_to_all | solution.py:133
  181.7 65.0 %all-to-all-start.1 = ((f32[33,16,2048]{2,0,1:T(8,128)}), f32[33,16,2048]{2,0,1:T(8,128)}, u32[]{:S(2)}, u32[]{:S(2)}) async-start(f32[33,16,2048]{2,0,1:T(8,128)} %copy.62), calls=%async_computation.1 | async-start | bytes 10485760 | tf_op jit(solution)/shard_map/all_to_all | solution.py:143
  246.7 65.0 %all-to-all-start.2 = ((f32[33,16,2048]{2,0,1:T(8,128)}), f32[33,16,2048]{2,0,1:T(8,128)}, u32[]{:S(2)}, u32[]{:S(2)}) async-start(f32[33,16,2048]{2,0,1:T(8,128)} %copy.64), calls=%async_computation.2 | async-start | bytes 10485760 | tf_op jit(solution)/shard_map/all_to_all | solution.py:144
  251.4 148.8 %all-reduce.3.cloned.1.call-start = ((), (), s32[]{:S(2)}) async-start(), calls=%async_computation.6 | async-start | bytes 524288 | tf_op jit(solution)/shard_map/psum | solution.py:157
  318.7 11.6 %slice-start = ((s8[4325376]{0:T(1024)(128)(4,1)}), s8[131072]{0:T(1024)(128)(4,1)S(1)}, s32[]{:S(2)}) async-start(s8[4325376]{0:T(1024)(128)(4,1)} %bitcast.118), calls=%async_computation.7 | async-start | bytes 262144
  324.1 6.2 slice-start.1
  324.1 10.7 %slice-start.2 = ((s8[4325376]{0:T(1024)(128)(4,1)}), s8[4194304]{0:T(1024)(128)(4,1)S(1)}, s32[]{:S(2)}) async-start(s8[4325376]{0:T(1024)(128)(4,1)} %bitcast.120), calls=%async_computation.9 | async-start | bytes 8388608
  330.3 4.4 slice-start.3
  364.5 41.9 %copy-start.2 = (f32[16,2,128,128]{3,2,1,0:T(8,128)}, f32[16,2,128,128]{3,2,1,0:T(8,128)S(1)}, u32[]{:S(2)}) copy-start(f32[16,2,128,128]{3,2,1,0:T(8,128)S(1)} %get-tuple-element.13) | copy-start | bytes 6291460
  400.2 4.0 copy-start.3
  400.2 4.0 copy-start.7
  404.2 2.2 copy-start.6
  413.4 2.2 copy-start.1
  436.4 57.3 %all-to-all-start.4 = ((f32[8,17,2,2048]{3,2,1,0:T(2,128)}), f32[8,17,2,2048]{3,2,1,0:T(2,128)}, u32[]{:S(2)}, u32[]{:S(2)}) async-start(f32[8,17,2,2048]{3,2,1,0:T(2,128)} %fusion.33), calls=%async_computation.4 | async-start | bytes 4456448 | tf_op jit(solution)/shard_map/all_to_all | solution.py:165
  493.7 32.4 %all-to-all-start.3 = ((f32[8,1,69632]{2,1,0:T(1,128)}), f32[8,1,69632]{2,1,0:T(1,128)}, u32[]{:S(2)}, u32[]{:S(2)}) async-start(f32[8,1,69632]{2,1,0:T(1,128)} %reshape.404), calls=%async_computation.3 | async-start | bytes 4456448 | tf_op jit(solution)/shard_map/all_to_all | solution.py:169
  597.0 3.2 copy-start
  626.1 1.5 copy-start.4
  626.1 1.5 copy-start.5
  626.1 1.5 copy-start.9
Sparse Core Ops, SparseCore 0:
  364.7 35.4 all-reduce.2
